TPU v7x, 256 devices: a whole 4x4x8 slice. The times are simulated.
256 devices in a mesh: ctx: 16 (over x, y_hi, core), tp: 16 (over z, y_lo).
Axes of the slice: x: 4, y: 4 (y_hi: 2, y_lo: 2; y = y_hi * 2 + y_lo), z: 8, core: 2. Of those that a mesh axis runs over, the one named last changes fastest.
Arguments:
- tokens: bfloat16 [2048, 4096], P('ctx', 'tp'), may hold values from -6 to 6
- gate_tiles: bfloat16 [1024, 128, 128], P('tp'), may hold values from -0.25 to 0.25
- up_tiles: bfloat16 [1024, 128, 128], P('tp'), may hold values from -0.25 to 0.25
- down_tiles: bfloat16 [1024, 128, 128], P('tp'), may hold values from -0.125 to 0.125
- gu_blocks: int32 [2, 1024], P(None, 'tp'), may hold values from 0 to 31, as said below
- down_blocks: int32 [2, 1024], P(None, 'tp'), may hold values from 0 to 31, as said below
- counts: int32 [2, 16], P(None, 'tp'), may hold values from 1 to 64, as said below
Outputs:
- mixed: bfloat16 [128, 16, 4096], P('tp', None, 'ctx')
Inputs may be any that keep to these rules, and one draw needn't show every extreme that they name: `gu_blocks`: within one shard's 64 slots the pairs (row 0, row 1) are all different; row 0 is below 32, row 1 below 8. `down_blocks`: within one shard's 64 slots the pairs (row 0, row 1) are all different; row 0 is below 8, row 1 below 32. In each row some shard has exactly 64 live slots; only the first counts slots of a shard are live.
All inputs are finite; a program needn't handle non-finite values.
Results may differ from a plain program's by a relative error of at most 0.0052.
Values may be sent and summed in bfloat16 or wider, within the bound.
No kernel may reach another device: no remote copies, remote signals or barrier semaphores. Data moves between devices by JAX's collectives and lax.ppermute only.
A program may use at most 64 MiB of HBM per device.

v0:
```python
import jax
import jax.numpy as jnp
from jax import lax
from jax.sharding import PartitionSpec as P

FF = 16384


def per_device(tokens, gate_tiles, up_tiles, down_tiles, gu_blocks, down_blocks, counts):
    gathered = lax.all_gather(tokens, "tp", axis=1, tiled=True)
    tok_rows, feat_width = gathered.shape
    slot_count = gate_tiles.shape[0]
    tile_size = gate_tiles.shape[1]
    in_blocks = feat_width // tile_size
    tp_count = lax.axis_size("tp")
    hid_blocks = FF // tp_count // tile_size
    widened = gathered.astype(jnp.float32)
    squares = jnp.mean(widened * widened, axis=1, keepdims=True)
    normed = (widened * lax.rsqrt(squares + 1e-05)).astype(jnp.bfloat16)
    slot_ids = jnp.arange(slot_count)
    valid_in = (slot_ids < counts[0, 0]).astype(jnp.float32)
    valid_out = (slot_ids < counts[1, 0]).astype(jnp.float32)
    pick_hidden = (gu_blocks[1][:, None] == jnp.arange(hid_blocks)[None, :]).astype(
        jnp.float32
    ) * valid_in[:, None]
    pick_out = (down_blocks[1][:, None] == jnp.arange(in_blocks)[None, :]).astype(
        jnp.float32
    ) * valid_out[:, None]
    block_rows = min(tok_rows, 512)

    def hidden_block(row_block):
        row_tiles = row_block.reshape(block_rows, in_blocks, tile_size)
        chosen = jnp.take(row_tiles, gu_blocks[0], axis=1)
        gate_part = jnp.einsum(
            "tmk,mkn->tmn", chosen, gate_tiles, preferred_element_type=jnp.float32
        )
        up_part = jnp.einsum("tmk,mkn->tmn", chosen, up_tiles, preferred_element_type=jnp.float32)
        gate_sum = jnp.einsum(
            "tmn,mh->thn", gate_part, pick_hidden, precision=lax.Precision.HIGHEST
        )
        up_sum = jnp.einsum("tmn,mh->thn", up_part, pick_hidden, precision=lax.Precision.HIGHEST)
        return (jax.nn.silu(gate_sum) * up_sum).astype(jnp.bfloat16)

    hidden = lax.map(hidden_block, normed.reshape(tok_rows // block_rows, block_rows, feat_width))
    hidden = hidden.reshape(tok_rows, hid_blocks, tile_size)
    first_shard = jnp.where(lax.axis_index("tp") == 0, 1.0, 0.0).astype(jnp.float32)
    chosen_hidden = jnp.take(hidden, down_blocks[0], axis=1)
    products = jnp.einsum(
        "tmk,mkn->tmn", chosen_hidden, down_tiles, preferred_element_type=jnp.float32
    )
    summed = jnp.einsum("tmn,mo->ton", products, pick_out, precision=lax.Precision.HIGHEST)
    partial_term = summed.reshape(tok_rows, feat_width) + first_shard * widened
    arrived = lax.all_to_all(
        partial_term.reshape(tok_rows, 1, feat_width),
        "ctx",
        split_axis=2,
        concat_axis=1,
        tiled=True,
    )
    finished = lax.psum_scatter(arrived, "tp", scatter_dimension=0, tiled=True)
    return finished.astype(jnp.bfloat16)


def solution(mesh):
    return jax.shard_map(
        per_device,
        mesh=mesh,
        in_specs=(
            P("ctx", "tp"),
            P("tp", None, None),
            P("tp", None, None),
            P("tp", None, None),
            P(None, "tp"),
            P(None, "tp"),
            P(None, "tp"),
        ),
        out_specs=P("tp", None, "ctx"),
        check_vma=False,
    )
```

profile of v0, /device:TPU:2, one launch (start us, length us, event | category | flops | bytes accessed | tf_op | source)
XLA Modules:
  0.0 236.4 jit_solution(7079399391941856147)
XLA Ops:
  6.5 1.7 copy.17
  8.3 1.3 fusion.53
  9.7 0.7 compare_convert_fusion
  10.9 0.7 fusion.45
  12.3 0.7 compare_and_fusion
  13.7 0.7 compare_and_fusion.1
  15.1 65.7 %all-gather.2.cloned.1.call-done = bf16[128,4096]{0,1:T(8,128)(2,1)} async-done(((bf16[128,256]{0,1:T(8,128)(2,1)}), bf16[128,4096]{0,1:T(8,128)(2,1)}) %all-gather.2.cloned.1.call-update) | async-done | bytes 1048592 | tf_op jit(solution)/shard_map/all_gather | solution.py:10
  80.8 1.8 fusion.6
  82.6 2.4 %fusion.7 = bf16[128,4096]{0,1:T(8,128)(2,1)} fusion(bf16[128,4096]{0,1:T(8,128)(2,1)} %all-gather.2.cloned.1.call-done, f32[128]{0:T(128)S(1)} %add_rsqrt_fusion), kind=kLoop, calls=%fused_computation.15 | loop fusion | flops 1572864 | bytes 2097664 | tf_op jit(solution)/shard_map/convert_element_type | solution.py:19
  85.0 1.6 copy.18
  86.6 2.2 gather_fusion
  88.8 2.5 %convolution_bitcast_fusion.2 = f32[128,64,128]{2,0,1:T(8,128)S(1)} fusion(bf16[64,128,128]{2,1,0:T(8,128)(2,1)S(1)} %copy-done, bf16[64,128,128]{2,1,0:T(8,128)(2,1)} %gather_fusion, pred[64]{0:T(512)(128)(4,1)S(1)} %compare_and_fusion), kind=kOutput, calls=%fused_computation.13 | convolution fusion | flops 269484032 | bytes 8388672 | tf_op jit(solution)/shard_map/while/body/eval_jaxpr/tmk,mkn->tmn/dot_general | solution.py:34
  91.6 0.8 convolution_bitcast_fusion.1
  92.4 4.4 %fusion.17 = f32[128,8,128]{2,1,0:T(8,128)S(1)} fusion(f32[128,64,128]{2,0,1:T(8,128)S(1)} %convolution_bitcast_fusion.2, f32[64]{0:T(128)S(1)} %compare_convert_fusion, s32[64]{0:T(128)S(1)} %slice_bitcast_fusion), kind=kOutput, calls=%fused_computation.24 | convolution fusion | flops 100664320 | bytes 4719104 | tf_op jit(solution)/shard_map/while/body/eval_jaxpr/tmn,mh->thn/dot_general | solution.py:38
  96.8 4.4 %fusion.26 = bf16[128,8,128]{2,1,0:T(8,128)(2,1)S(1)} fusion(f32[128,64,128]{2,0,1:T(8,128)S(1)} %convolution_bitcast_fusion.1, f32[128,8,128]{2,1,0:T(8,128)S(1)} %fusion.17, f32[64]{0:T(128)S(1)} %compare_convert_fusion, s32[64]{0:T(128)S(1)} %slice_bitcast_fusion), kind=kOutput, calls=%fused_computation.27 | convolution fusion | flops 101450752 | bytes 4981248 | tf_op jit(solution)/shard_map/while/body/eval_jaxpr/tmn,mh->thn/dot_general | solution.py:41
  101.2 2.2 gather_fusion.1
  103.3 3.0 %convolution_bitcast_fusion = f32[128,64,128]{2,0,1:T(8,128)S(1)} fusion(bf16[64,128,128]{2,1,0:T(8,128)(2,1)} %param.10, bf16[64,128,128]{2,1,0:T(8,128)(2,1)} %gather_fusion.1, pred[64]{0:T(512)(128)(4,1)S(1)} %compare_and_fusion.1), kind=kOutput, calls=%fused_computation.11 | convolution fusion | flops 269484032 | bytes 8388672 | tf_op jit(solution)/shard_map/tmk,mkn->tmn/dot_general | solution.py:48
  106.3 6.0 %fusion.14 = f32[128,32,128]{2,1,0:T(8,128)} fusion(f32[128,64,128]{2,0,1:T(8,128)S(1)} %convolution_bitcast_fusion, f32[64]{0:T(128)S(1)} %compare_convert_fusion.1, s32[64]{0:T(128)S(1)} %slice_bitcast_fusion.1), kind=kOutput, calls=%fused_computation.23 | convolution fusion | flops 402657280 | bytes 6291968 | tf_op jit(solution)/shard_map/tmn,mo->ton/dot_general | solution.py:51
  112.3 3.1 %copy.26 = f32[128,32,128]{0,2,1:T(8,128)} copy(f32[128,32,128]{2,1,0:T(8,128)} %fusion.14) | data formatting | bytes 4194304 | tf_op jit(solution)/shard_map/reshape | solution.py:52
  115.4 1.8 fusion.8
  117.2 33.9 %all_to_all.12 = f32[128,1,4096]{0,1,2:T(1,128)} all-to-all(f32[128,1,4096]{0,1,2:T(1,128)S(1)} %bitcast.60), channel_id=1, replica_groups=mesh['ctx'=16,'tp'=16] {'ctx'}, dimensions={2} | all-to-all | bytes 4194304 | tf_op jit(solution)/shard_map/all_to_all | solution.py:53
  151.1 3.1 %copy.25 = f32[128,16,256]{2,1,0:T(8,128)} copy(f32[128,16,256]{0,2,1:T(8,128)} %bitcast.61) | data formatting | bytes 4194304 | tf_op jit(solution)/shard_map/all_to_all | solution.py:53
  154.2 73.8 %reduce-scatter.2.cloned.1.call-done = f32[8,16,256]{2,1,0:T(8,128)} async-done(((f32[128,16,256]{2,1,0:T(8,128)}), f32[8,16,256]{2,1,0:T(8,128)}) %reduce-scatter.2.cloned.1.call-update) | async-done | bytes 131088 | tf_op jit(solution)/shard_map/reduce_scatter | solution.py:60
  228.0 1.5 convert_element_type.34
  (20 shorter events, 3.1 us)
Async XLA Ops:
  6.5 82.2 %copy-start = (bf16[64,128,128]{2,1,0:T(8,128)(2,1)S(1)}, bf16[64,128,128]{2,1,0:T(8,128)(2,1)}, u32[]{:S(2)}) copy-start(bf16[64,128,128]{2,1,0:T(8,128)(2,1)} %param.8) | copy-start | bytes 6291460
  6.5 74.2 %all-gather.2.cloned.1.call-start = ((), (), s32[]{:S(2)}) async-start(), calls=%async_computation.2 | async-start | bytes 1114112 | tf_op jit(solution)/shard_map/all_gather | solution.py:10
  8.3 219.7 %reduce-scatter.2.cloned.1.call-start = ((), (), s32[]{:S(2)}) async-start(), calls=%async_computation.3 | async-start | bytes 2228224 | tf_op jit(solution)/shard_map/reduce_scatter | solution.py:60
  88.8 2.5 %copy-start.1 = (bf16[64,128,128]{2,1,0:T(8,128)(2,1)S(1)}, bf16[64,128,128]{2,1,0:T(8,128)(2,1)}, u32[]{:S(2)}) copy-start(bf16[64,128,128]{2,1,0:T(8,128)(2,1)} %gather_fusion) | copy-start | bytes 6291460
  88.8 2.9 %copy-start.3 = (bf16[64,128,128]{2,1,0:T(8,128)(2,1)S(1)}, bf16[64,128,128]{2,1,0:T(8,128)(2,1)}, u32[]{:S(2)}) copy-start(bf16[64,128,128]{2,1,0:T(8,128)(2,1)} %param.9) | copy-start | bytes 6291460
  112.3 3.1 %copy-start.2 = (bf16[128,4096]{0,1:T(8,128)(2,1)S(1)}, bf16[128,4096]{0,1:T(8,128)(2,1)}, u32[]{:S(2)}) copy-start(bf16[128,4096]{0,1:T(8,128)(2,1)} %all-gather.2.cloned.1.call-done) | copy-start | bytes 3145732
Sparse Core Ops, SparseCore 0:
  9.1 71.5 all-gather.1
  154.4 73.5 reduce-scatter.1
where the time goes:
time: 237 us; the launch traced here: 236 us
  waiting for transfers between devices  140 us (59%)
  blocking collectives  33.9 us (14%)
  matrix products  21 us (9%)
  local copies, waits for them, and re-layouts  16.9 us (7%)
  between operations  13.5 us (6%)
  other arithmetic  11.5 us (5%)
    reduce_scatter x1, waiting for transfers between devices, per_device(): finished = lax.psum_scatter(arrived, 'tp', scatter_dimension=0, tiled=True)  73.8 us
    all_gather x1, waiting for transfers between devices, per_device(): gathered = lax.all_gather(tokens, 'tp', axis=1, tiled=True)  65.7 us
    all_to_all x1, blocking collectives, per_device(): lax.all_to_all(partial_term.reshape(tok_rows, 1, feat_width), 'ctx', spli...  33.9 us
    dot_general x1, matrix products, per_device(): jnp.einsum('tmn,mo->ton', products, pick_out, precision=lax.Precision.HIG...  6 us
  transfers between devices with their start and end apart: 2, of which 2 were waited for; matrix products, arithmetic and copies ran while one was open for 3% of the time, Pallas kernels for 0%

commit v1 on v0

--- a/solution.py
+++ b/solution.py
@@ -6,8 +6,15 @@
 FF = 16384
 
 
+def swapped_in(value, mesh_axis, dim):
+    count = lax.axis_size(mesh_axis)
+    blocks = jnp.stack([value for _ in range(count)])
+    blocks = lax.all_to_all(blocks, mesh_axis, split_axis=0, concat_axis=0)
+    return jnp.concatenate(blocks, axis=dim)
+
+
 def per_device(tokens, gate_tiles, up_tiles, down_tiles, gu_blocks, down_blocks, counts):
-    gathered = lax.all_gather(tokens, "tp", axis=1, tiled=True)
+    gathered = swapped_in(tokens, "tp", 1)
     tok_rows, feat_width = gathered.shape
     slot_count = gate_tiles.shape[0]
     tile_size = gate_tiles.shape[1]

time: 237 us -> 212 us (0.89)
  waiting for transfers between devices: 140 us -> 96.6 us
  starting transfers between devices: 0.04 us -> 9.62 us
  local copies, waits for them, and re-layouts: 16.9 us -> 24.8 us
    all_gather x1 -> x0, waiting for transfers between devices: 65.7 us -> none  [per_device(): gathered = lax.all_gather(tokens, 'tp', axis=1, tiled=True)]
    all_to_all x0 -> x1, waiting for transfers between devices: none -> 26.6 us  [swapped_in(): blocks = lax.all_to_all(blocks, mesh_axis, split_axis=0, concat_axis=0)]
    all_to_all x0 -> x1, starting transfers between devices: none -> 9.58 us  [swapped_in(): blocks = lax.all_to_all(blocks, mesh_axis, split_axis=0, concat_axis=0)]
    add x0 -> x1, local copies, waits for them, and re-layouts: none -> 5.63 us  [per_device(): partial_term = summed.reshape(tok_rows, feat_width) + first_shard * widened]
    reduce_scatter x1, waiting for transfers between devices: 73.8 us -> 70 us  [per_device(): finished = lax.psum_scatter(arrived, 'tp', scatter_dimension=0, tiled=True)]
    convert_element_type x0 -> x1, local copies, waits for them, and re-layouts: none -> 2.92 us  [per_device(): widened = gathered.astype(jnp.float32)]
    mul x0 -> x1, local copies, waits for them, and re-layouts: none -> 2.92 us  [per_device(): partial_term = summed.reshape(tok_rows, feat_width) + first_shard * widened]
  transfers between devices with their start and end apart: 2 -> 2, of which waited for: 2 -> 2; matrix products, arithmetic and copies ran while one was open for 3% -> 1% of each run, Pallas kernels for 0% -> 0%
where the time goes in v1:
time: 212 us
  waiting for transfers between devices  96.6 us (46%)
  blocking collectives  34.1 us (16%)
  local copies, waits for them, and re-layouts  24.8 us (12%)
  matrix products  21 us (10%)
  between operations  13.6 us (6%)
  other arithmetic  11.9 us (6%)
  starting transfers between devices  9.62 us (5%)
    reduce_scatter x1, waiting for transfers between devices, per_device(): finished = lax.psum_scatter(arrived, 'tp', scatter_dimension=0, tiled=True)  70 us
    all_to_all x1, blocking collectives, per_device(): lax.all_to_all(partial_term.reshape(tok_rows, 1, feat_width), 'ctx', spli...  34.1 us
    all_to_all x1, waiting for transfers between devices, swapped_in(): blocks = lax.all_to_all(blocks, mesh_axis, split_axis=0, concat_axis=0)  26.6 us
    all_to_all x1, starting transfers between devices, swapped_in(): blocks = lax.all_to_all(blocks, mesh_axis, split_axis=0, concat_axis=0)  9.58 us
    dot_general x1, matrix products, per_device(): jnp.einsum('tmn,mo->ton', products, pick_out, precision=lax.Precision.HIG...  6.04 us
    add x1, local copies, waits for them, and re-layouts, per_device(): partial_term = summed.reshape(tok_rows, feat_width) + first_shard * widened  5.63 us
    dot_general x1, matrix products, hidden_block(): jnp.einsum('tmn,mh->thn', gate_part, pick_hidden, precision=lax.Precision...  4.37 us
    dot_general x1, matrix products, hidden_block(): jnp.einsum('tmn,mh->thn', up_part, pick_hidden, precision=lax.Precision.H...  4.36 us
  transfers between devices with their start and end apart: 2, of which 2 were waited for; matrix products, arithmetic and copies ran while one was open for 1% of the time, Pallas kernels for 0%

profile of v1, /device:TPU:2, one launch (start us, length us, event | category | flops | bytes accessed | tf_op | source)
XLA Modules:
  0.0 211.7 jit_solution(6531631444712358306)
XLA Ops:
  6.5 1.1 copy.25
  7.6 1.2 stack.2
  8.8 9.6 %all-to-all-start = ((bf16[16,128,256]{1,2,0:T(8,128)(2,1)}), bf16[16,128,256]{1,2,0:T(8,128)(2,1)S(1)}, u32[]{:S(2)}, u32[]{:S(2)}) async-start(bf16[16,128,256]{1,2,0:T(8,128)(2,1)} %stack.2), calls=%async_computation | async-start | bytes 2097152 | tf_op jit(solution)/shard_map/all_to_all | solution.py:12
  20.5 26.6 %all-to-all-done = bf16[16,128,256]{1,2,0:T(8,128)(2,1)S(1)} async-done(((bf16[16,128,256]{1,2,0:T(8,128)(2,1)}), bf16[16,128,256]{1,2,0:T(8,128)(2,1)S(1)}, u32[]{:S(2)}, u32[]{:S(2)}) %all-to-all-start) | async-done | bytes 1048608 | tf_op jit(solution)/shard_map/all_to_all | solution.py:12
  47.1 1.8 convert_multiply_fusion
  48.9 1.5 convert_element_type.60
  50.4 2.9 %copy.26 = f32[128,32,128]{2,0,1:T(8,128)} copy(f32[128,32,128]{0,2,1:T(8,128)} %bitcast.61) | data formatting | bytes 4194304 | tf_op jit(solution)/shard_map/convert_element_type | solution.py:24
  53.4 1.9 multiply_convert_fusion
  55.3 2.1 %gather_fusion = bf16[64,128,128]{2,1,0:T(8,128)(2,1)} fusion(bf16[128,32,128]{2,0,1:T(8,128)(2,1)S(1)} %multiply_convert_fusion, s32[1024]{0:T(1024)S(1)} %pad_clamp_fusion.1), kind=kCustom, calls=%fused_computation | custom fusion | bytes 4194560 | tf_op jit(solution)/shard_map/while/body/eval_jaxpr/jit(_take)/gather | solution.py:40
  57.4 2.5 %convolution_bitcast_fusion.2 = f32[128,64,128]{2,0,1:T(8,128)S(1)} fusion(bf16[64,128,128]{2,1,0:T(8,128)(2,1)S(1)} %copy-done, bf16[64,128,128]{2,1,0:T(8,128)(2,1)} %gather_fusion, pred[64]{0:T(512)(128)(4,1)S(1)} %compare_and_fusion), kind=kOutput, calls=%fused_computation.10 | convolution fusion | flops 269484032 | bytes 8388672 | tf_op jit(solution)/shard_map/while/body/eval_jaxpr/tmk,mkn->tmn/dot_general | solution.py:41
  60.3 0.8 convolution_bitcast_fusion.1
  61.1 4.4 %fusion.14 = f32[128,8,128]{2,1,0:T(8,128)S(1)} fusion(f32[128,64,128]{2,0,1:T(8,128)S(1)} %convolution_bitcast_fusion.2, f32[64]{0:T(128)S(1)} %compare_convert_fusion, s32[64]{0:T(128)S(1)} %slice_bitcast_fusion), kind=kOutput, calls=%fused_computation.20 | convolution fusion | flops 100664320 | bytes 4719104 | tf_op jit(solution)/shard_map/while/body/eval_jaxpr/tmn,mh->thn/dot_general | solution.py:45
  65.4 4.4 %fusion.23 = bf16[128,8,128]{2,1,0:T(8,128)(2,1)S(1)} fusion(f32[128,64,128]{2,0,1:T(8,128)S(1)} %convolution_bitcast_fusion.1, f32[128,8,128]{2,1,0:T(8,128)S(1)} %fusion.14, f32[64]{0:T(128)S(1)} %compare_convert_fusion, s32[64]{0:T(128)S(1)} %slice_bitcast_fusion), kind=kOutput, calls=%fused_computation.23 | convolution fusion | flops 101450752 | bytes 4981248 | tf_op jit(solution)/shard_map/while/body/eval_jaxpr/tmn,mh->thn/dot_general | solution.py:48
  69.8 2.1 %gather_fusion.1 = bf16[64,128,128]{2,1,0:T(8,128)(2,1)} fusion(bf16[128,8,128]{2,0,1:T(8,128)(2,1)S(1)} %copy.29, s32[1024]{0:T(1024)S(1)} %pad_clamp_fusion), kind=kCustom, calls=%fused_computation.1 | custom fusion | bytes 4194560 | tf_op jit(solution)/shard_map/jit(_take)/gather | solution.py:54
  72.0 3.0 %convolution_bitcast_fusion = f32[128,64,128]{2,0,1:T(8,128)S(1)} fusion(bf16[64,128,128]{2,1,0:T(8,128)(2,1)} %param.10, bf16[64,128,128]{2,1,0:T(8,128)(2,1)} %gather_fusion.1, pred[64]{0:T(512)(128)(4,1)S(1)} %compare_and_fusion.1), kind=kOutput, calls=%fused_computation.8 | convolution fusion | flops 269484032 | bytes 8388672 | tf_op jit(solution)/shard_map/tmk,mkn->tmn/dot_general | solution.py:55
  74.9 6.0 %fusion.11 = f32[128,32,128]{2,1,0:T(8,128)} fusion(f32[128,64,128]{2,0,1:T(8,128)S(1)} %convolution_bitcast_fusion, f32[64]{0:T(128)S(1)} %compare_convert_fusion.1, s32[64]{0:T(128)S(1)} %slice_bitcast_fusion.1), kind=kOutput, calls=%fused_computation.19 | convolution fusion | flops 402657280 | bytes 6291968 | tf_op jit(solution)/shard_map/tmn,mo->ton/dot_general | solution.py:58
  81.0 2.7 %reshape.140 = f32[128,1,4096]{2,0,1:T(8,128)} reshape(f32[128,32,128]{2,1,0:T(8,128)} %fusion.11) | data formatting | bytes 4194304 | tf_op jit(solution)/shard_map/reshape | solution.py:59
  83.7 2.9 %copy.34 = f32[128,1,4096]{2,0,1:T(8,128)} copy(f32[128,1,4096]{0,2,1:T(8,128)} %bitcast.60) | data formatting | bytes 4194304 | tf_op jit(solution)/shard_map/mul | solution.py:59
  86.6 3.8 %add.85 = f32[128,1,4096]{2,0,1:T(8,128)} add(f32[128,1,4096]{2,0,1:T(8,128)} %reshape.140, f32[128,1,4096]{2,0,1:T(8,128)} %copy.34) | non-fusion elementwise | flops 524288 | bytes 6291456 | tf_op jit(solution)/shard_map/add | solution.py:59
  90.4 5.6 %copy.32 = f32[128,1,4096]{0,1,2:T(1,128)} copy(f32[128,1,4096]{2,0,1:T(8,128)} %add.85) | data formatting | bytes 4194304 | tf_op jit(solution)/shard_map/add | solution.py:59
  96.1 34.1 %all_to_all.17 = f32[128,1,4096]{0,1,2:T(1,128)} all-to-all(f32[128,1,4096]{0,1,2:T(1,128)} %copy.32), channel_id=1, replica_groups=mesh['ctx'=16,'tp'=16] {'ctx'}, dimensions={2} | all-to-all | bytes 4194304 | tf_op jit(solution)/shard_map/all_to_all | solution.py:60
  130.2 3.1 %copy.33 = f32[128,16,256]{2,1,0:T(8,128)} copy(f32[128,16,256]{0,2,1:T(8,128)} %bitcast.62) | data formatting | bytes 4194304 | tf_op jit(solution)/shard_map/all_to_all | solution.py:60
  133.3 70.0 %reduce-scatter.2.cloned.1.call-done = f32[8,16,256]{2,1,0:T(8,128)} async-done(((f32[128,16,256]{2,1,0:T(8,128)}), f32[8,16,256]{2,1,0:T(8,128)}) %reduce-scatter.2.cloned.1.call-update) | async-done | bytes 131088 | tf_op jit(solution)/shard_map/reduce_scatter | solution.py:67
  203.3 1.5 convert_element_type.58
  (27 shorter events, 2.3 us)
Async XLA Ops:
  6.5 50.9 %copy-start = (bf16[64,128,128]{2,1,0:T(8,128)(2,1)S(1)}, bf16[64,128,128]{2,1,0:T(8,128)(2,1)}, u32[]{:S(2)}) copy-start(bf16[64,128,128]{2,1,0:T(8,128)(2,1)} %param.8) | copy-start | bytes 6291460
  6.5 11.9 %copy-start.3 = (s32[2,1]{0,1:T(1,128)S(1)}, s32[2,1]{0,1:T(1,128)}, u32[]{:S(2)}) copy-start(s32[2,1]{0,1:T(1,128)} %param.13) | copy-start | bytes 28
  6.5 13.8 %copy-start.4 = (s32[2,64]{1,0:T(2,128)S(1)}, s32[2,64]{1,0:T(2,128)}, u32[]{:S(2)}) copy-start(s32[2,64]{1,0:T(2,128)} %param.11) | copy-start | bytes 1540
  6.5 13.8 %copy-start.5 = (s32[2,64]{1,0:T(2,128)S(1)}, s32[2,64]{1,0:T(2,128)}, u32[]{:S(2)}) copy-start(s32[2,64]{1,0:T(2,128)} %param.12) | copy-start | bytes 1540
  8.8 38.3 %all-to-all-start = ((bf16[16,128,256]{1,2,0:T(8,128)(2,1)}), bf16[16,128,256]{1,2,0:T(8,128)(2,1)S(1)}, u32[]{:S(2)}, u32[]{:S(2)}) async-start(bf16[16,128,256]{1,2,0:T(8,128)(2,1)} %stack.2), calls=%async_computation | async-start | bytes 2097152 | tf_op jit(solution)/shard_map/all_to_all | solution.py:12
  18.4 184.9 %reduce-scatter.2.cloned.1.call-start = ((), (), s32[]{:S(2)}) async-start(), calls=%async_computation.3 | async-start | bytes 2228224 | tf_op jit(solution)/shard_map/reduce_scatter | solution.py:67
  57.4 2.5 %copy-start.1 = (bf16[64,128,128]{2,1,0:T(8,128)(2,1)S(1)}, bf16[64,128,128]{2,1,0:T(8,128)(2,1)}, u32[]{:S(2)}) copy-start(bf16[64,128,128]{2,1,0:T(8,128)(2,1)} %gather_fusion) | copy-start | bytes 6291460
  57.4 2.9 %copy-start.2 = (bf16[64,128,128]{2,1,0:T(8,128)(2,1)S(1)}, bf16[64,128,128]{2,1,0:T(8,128)(2,1)}, u32[]{:S(2)}) copy-start(bf16[64,128,128]{2,1,0:T(8,128)(2,1)} %param.9) | copy-start | bytes 6291460
Sparse Core Ops, SparseCore 0:
  133.5 69.8 reduce-scatter.1
